TPU v7x, 128 devices: a whole 4x4x4 slice. The times are simulated.
128 devices in a mesh: row: 4 (over y), vocab: 32 (over z, x, core).
Axes of the slice: x: 4, y: 4, z: 4, core: 2. Of those that a mesh axis runs over, the one named last changes fastest.
Arguments:
- tokens: bfloat16 [1280, 7168], P(('row', 'vocab')), may hold values from -60 to 60
- norm_gain: float32 [7168], replicated, may hold values from 0.5 to 1.5
- router: bfloat16 [7168, 32], replicated, may hold values from -0.0625 to 0.0625
- routes: int32 [1280, 8], P(('row', 'vocab')), may hold values from 0 to 31, all different within a row; in each aligned block of 10 rows (0 to 9, 10 to 19, ...) at most 3 rows name the same one
- w_gate: bfloat16 [32, 7168, 1024], P('vocab', None, 'row'), may hold values from -0.0625 to 0.0625
- w_up: bfloat16 [32, 7168, 1024], P('vocab', None, 'row'), may hold values from -0.0625 to 0.0625
- w_down: bfloat16 [32, 1024, 7168], P('vocab', 'row'), may hold values from -0.1875 to 0.1875
- head_gain: float32 [7168], replicated, may hold values from 0.5 to 1.5
- head: bfloat16 [65536, 7168], P(('row', 'vocab')), may hold values from -0.18 to 0.18
- draft_logits: bfloat16 [256, 4, 65536], P(None, None, ('row', 'vocab')), may hold values from -18 to 235
- draft_tokens: int32 [256, 4], replicated, may hold values from 0 to 65535
- reject_pos: int32 [256], replicated, may hold values from 0 to 4
Outputs:
- residual: float32 [256, 65536], P(None, ('row', 'vocab'))
- accept: float32 [256, 4], replicated
Inputs may be any that keep to these rules, and one draw needn't show every extreme that they name: `routes`: each row names 8 different experts. Among the rows of one device no expert is named more than 3 times, and some device's rows name some expert exactly 3 times.
All inputs are finite; a program needn't handle non-finite values.
Results may differ from a plain program's by a relative error of at most 0.012.
Values may be sent and summed in bfloat16 or wider, within the bound.
No kernel may reach another device: no remote copies, remote signals or barrier semaphores. Data moves between devices by JAX's collectives and lax.ppermute only.
A program may use at most 256 MiB of HBM per device.

v0:
```python
import jax
import jax.numpy as jnp
from jax import lax
from jax.sharding import PartitionSpec as P

V = 65536
DRAFTS = 4


def rms_norm(values, gain):
    return values * lax.rsqrt(jnp.mean(values * values, axis=-1, keepdims=True) + 1e-06) * gain


def body(
    tokens,
    norm_gain,
    router,
    routes,
    w_gate,
    w_up,
    w_down,
    head_gain,
    head,
    draft_logits,
    draft_tokens,
    reject_pos,
):
    vocab_count = lax.axis_size("vocab")
    rows_dev = tokens.shape[0]
    model_width = tokens.shape[1]
    top_k = routes.shape[1]
    experts = w_gate.shape[0] * vocab_count
    capacity = min(rows_dev, (rows_dev * top_k + experts - 1) // experts)
    ff_part = w_gate.shape[2]
    resid_in = tokens.astype(jnp.float32)
    normed = rms_norm(resid_in, norm_gain).astype(jnp.bfloat16)
    scores = jax.nn.sigmoid(jnp.dot(normed, router, preferred_element_type=jnp.float32))
    member = routes[:, :, None] == jnp.arange(experts, dtype=jnp.int32)[None, None, :]
    chosen = jnp.any(member, axis=1)
    chosen_int = chosen.astype(jnp.int32)
    picked = chosen.astype(jnp.float32) * scores
    weights = 2.5 * picked / jnp.sum(picked, axis=1, keepdims=True)
    earlier = jnp.cumsum(chosen_int, axis=0) - chosen_int
    slot_ids = jnp.arange(capacity, dtype=jnp.int32)[None, :, None]
    selector = ((earlier.T[:, None, :] == slot_ids) & chosen.T[:, None, :]).astype(jnp.float32)
    send_buffer = jnp.einsum(
        "esr,rd->esd", selector.astype(jnp.bfloat16), normed, preferred_element_type=jnp.float32
    ).astype(jnp.bfloat16)
    gate_w = w_gate[0]
    up_w = w_up[0]
    down_w = w_down[0]
    received = lax.all_to_all(send_buffer, "vocab", split_axis=0, concat_axis=0, tiled=True)
    slot_count = received.shape[1]
    shard_piece = lax.all_gather(received, "row", axis=0, tiled=True)
    flat_rows = shard_piece.reshape(-1, model_width)
    gate_out = jnp.dot(flat_rows, gate_w, preferred_element_type=jnp.float32)
    up_out = jnp.dot(flat_rows, up_w, preferred_element_type=jnp.float32)
    hidden_hidden = (jax.nn.silu(gate_out) * up_out).astype(jnp.bfloat16)
    hidden = hidden_hidden.reshape(shard_piece.shape[0], shard_piece.shape[1], ff_part)
    down_out = jnp.dot(hidden.reshape(-1, ff_part), down_w, preferred_element_type=jnp.float32)
    down_out = down_out.astype(jnp.bfloat16).astype(jnp.float32)
    summed = lax.psum_scatter(
        down_out.reshape(received.shape[0] * lax.axis_size("row"), slot_count, model_width).astype(
            jnp.bfloat16
        ),
        "row",
        scatter_dimension=0,
        tiled=True,
    )
    returned = lax.all_to_all(summed, "vocab", split_axis=0, concat_axis=0, tiled=True)
    combine = selector * weights.T[:, None, :]
    moe_sum = jnp.einsum(
        "esr,esd->rd", combine, returned.astype(jnp.float32), precision=lax.Precision.HIGHEST
    )
    mixed_rows = resid_in + moe_sum
    final_normed = rms_norm(mixed_rows, head_gain).astype(jnp.bfloat16)
    local_vocab = head.shape[0]
    logits = lax.dot_general(
        lax.all_gather(final_normed, ("row", "vocab"), axis=0, tiled=True),
        head,
        (((1,), (1,)), ((), ())),
        preferred_element_type=jnp.float32,
    )
    requests = draft_tokens.shape[0]
    slot_total = DRAFTS + 1
    target_logits = logits.reshape(requests, slot_total, local_vocab)
    draft_vals = draft_logits.astype(jnp.float32)
    offset = lax.axis_index(("row", "vocab")) * local_vocab
    local_ids = draft_tokens - offset
    id_match = jnp.arange(local_vocab, dtype=jnp.int32)[None, None, :] == local_ids[:, :, None]
    pick_target = jnp.sum(jnp.where(id_match, target_logits[:, :DRAFTS], 0.0), axis=-1)
    pick_draft = jnp.sum(jnp.where(id_match, draft_vals, 0.0), axis=-1)
    local_top_target = jnp.max(target_logits, axis=-1)
    local_top_draft = jnp.max(draft_vals, axis=-1)
    top_target, top_draft = lax.pmax((local_top_target, local_top_draft), ("row", "vocab"))
    local_sum_target = jnp.sum(jnp.exp(target_logits - top_target[:, :, None]), axis=-1)
    local_sum_draft = jnp.sum(jnp.exp(draft_vals - top_draft[:, :, None]), axis=-1)
    sum_target, sum_draft, pick_t, pick_d = lax.psum(
        (local_sum_target, local_sum_draft, pick_target, pick_draft), ("row", "vocab")
    )
    target = jnp.exp(target_logits - top_target[:, :, None]) / sum_target[:, :, None]
    draft_prob = jnp.exp(draft_vals - top_draft[:, :, None]) / sum_draft[:, :, None]
    log_target = pick_t - top_target[:, :DRAFTS] - jnp.log(sum_target[:, :DRAFTS])
    log_draft = pick_d - top_draft - jnp.log(sum_draft)
    accept = jnp.exp(jnp.minimum(log_target - log_draft, 0.0))
    position = (jnp.arange(slot_total, dtype=jnp.int32)[None, :] == reject_pos[:, None]).astype(
        jnp.float32
    )
    target_at = jnp.sum(position[:, :, None] * target, axis=1)
    draft_at = jnp.sum(position[:, :DRAFTS, None] * draft_prob, axis=1)
    gap_rows = jnp.maximum(target_at - draft_at, 0.0)
    gap_total = lax.psum(jnp.sum(gap_rows, axis=-1), ("row", "vocab"))
    residual = jnp.sqrt(V * gap_rows / gap_total[:, None])
    return (residual, accept)


def solution(mesh):
    placed = (
        P(("row", "vocab"), None),
        P(),
        P(),
        P(("row", "vocab"), None),
        P("vocab", None, "row"),
        P("vocab", None, "row"),
        P("vocab", "row", None),
        P(),
        P(("row", "vocab"), None),
        P(None, None, ("row", "vocab")),
        P(),
        P(),
    )
    return jax.shard_map(
        body,
        mesh=mesh,
        in_specs=placed,
        out_specs=(P(None, ("row", "vocab")), P()),
        check_vma=False,
    )
```

profile of v0, /device:TPU:0, one launch (start us, length us, event | category | flops | bytes accessed | tf_op | source)
XLA Modules:
  0.0 697.8 jit_solution(13152813386539640018)
XLA Ops:
  7.2 0.0 copy-start
  7.2 0.0 all-gather.4.cloned.1.call-start
  7.2 0.8 copy.38
  8.0 0.1 fusion.36
  8.2 1.1 fusion.23
  9.3 1.5 convolution_convert_fusion.1
  10.8 1.2 copy.39
  12.0 33.8 %all_to_all.10 = bf16[32,3,7168]{2,1,0:T(4,128)(2,1)S(1)} all-to-all(bf16[32,3,7168]{2,1,0:T(4,128)(2,1)S(1)} %copy.39), channel_id=1, replica_groups=mesh['row'=4,'vocab'=32] {'vocab'}, dimensions={0} | all-to-all | bytes 2752512 | tf_op jit(solution)/shard_map/all_to_all | solution.py:52
  45.8 1.6 copy.40
  47.5 0.0 all-gather.4.cloned.1.call-update
  47.5 0.2 all-reduce.6.cloned.1.call-start
  47.7 56.8 %all-gather.4.cloned.1.call-done = bf16[128,3,7168]{2,0,1:T(8,128)(2,1)} async-done(((bf16[32,3,7168]{2,0,1:T(8,128)(2,1)}), bf16[128,3,7168]{2,0,1:T(8,128)(2,1)}) %all-gather.4.cloned.1.call-update) | async-done | bytes 5505040 | tf_op jit(solution)/shard_map/all_gather | solution.py:54
  104.5 10.2 %copy.41 = bf16[128,3,7168]{2,1,0:T(4,128)(2,1)} copy(bf16[128,3,7168]{2,0,1:T(8,128)(2,1)} %all-gather.4.cloned.1.call-done) | data formatting | bytes 11010048 | tf_op jit(solution)/shard_map/all_gather | solution.py:54
  114.8 13.0 %reshape.67 = bf16[384,7168]{1,0:T(8,128)(2,1)} reshape(bf16[128,3,7168]{2,1,0:T(4,128)(2,1)} %copy.41) | data formatting | bytes 11010048 | tf_op jit(solution)/shard_map/reshape | solution.py:55
  127.8 5.4 fusion.4
  133.2 0.0 copy-done.5
  133.2 0.9 copy-done.12
  134.2 1.6 fusion.17
  135.8 0.4 copy-done.6
  136.2 4.0 convolution_convert_fusion
  140.2 12.3 %convert_element_type.57 = bf16[128,3,7168]{2,1,0:T(4,128)(2,1)} reshape(bf16[384,7168]{1,0:T(8,128)(2,1)} %convolution_convert_fusion) | data formatting | bytes 11010048 | tf_op jit(solution)/shard_map/convert_element_type | solution.py:63
  152.5 0.0 all-reduce.6.cloned.1.call-update
  152.5 0.6 copy-done.13
  153.2 0.6 dynamic-slice
  154.4 0.0 copy-start.8
  154.4 142.7 %all-reduce.6.cloned.1.call-done = bf16[128,3,7168]{2,1,0:T(4,128)(2,1)} async-done(((bf16[128,3,7168]{2,1,0:T(4,128)(2,1)}), bf16[128,3,7168]{2,1,0:T(4,128)(2,1)}) %all-reduce.6.cloned.1.call-update) | async-done | bytes 5505040
  297.1 3.5 constant_dynamic-slice_fusion
  300.6 7.4 %all-to-all-start.1 = ((bf16[32,3,7168]{2,1,0:T(4,128)(2,1)}), bf16[32,3,7168]{2,1,0:T(4,128)(2,1)S(1)}, u32[]{:S(2)}, u32[]{:S(2)}) async-start(bf16[32,3,7168]{2,1,0:T(4,128)(2,1)} %constant_dynamic-slice_fusion), calls=%async_computation.1 | async-start | bytes 3670016 | tf_op jit(solution)/shard_map/all_to_all | solution.py:70
  308.0 0.3 all-gather.6.cloned.1.call-start
  308.2 0.0 copy-done
  308.2 0.0 copy-done.8
  308.2 1.4 select_reduce_fusion
  309.6 0.1 fusion.47
  309.7 25.3 %all-to-all-done.1 = bf16[32,3,7168]{2,1,0:T(4,128)(2,1)S(1)} async-done(((bf16[32,3,7168]{2,1,0:T(4,128)(2,1)}), bf16[32,3,7168]{2,1,0:T(4,128)(2,1)S(1)}, u32[]{:S(2)}, u32[]{:S(2)}) %all-to-all-start.1) | async-done | bytes 1376288 | tf_op jit(solution)/shard_map/all_to_all | solution.py:70
  335.0 2.3 multiply_reduce_fusion.1
  337.3 0.0 copy-done.9
  337.3 0.8 fusion.26
  338.1 0.0 all-gather.6.cloned.1.call-update
  338.1 0.0 copy-done.10
  338.2 0.8 copy.43
  339.0 0.0 copy-done.3
  339.0 0.5 reduce_max.27
  339.5 0.0 copy-done.11
  339.5 0.1 fusion.33
  339.6 94.2 %all-gather.6.cloned.1.call-done = bf16[128,10,7168]{2,1,0:T(8,128)(2,1)} async-done(((bf16[1,10,7168]{2,1,0:T(8,128)(2,1)}), bf16[128,10,7168]{2,1,0:T(8,128)(2,1)}) %all-gather.6.cloned.1.call-update) | async-done | bytes 18350096 | tf_op jit(solution)/shard_map/all_gather | solution.py:79
  433.8 28.2 %reshape.70 = bf16[1280,7168]{1,0:T(8,128)(2,1)} reshape(bf16[128,10,7168]{2,1,0:T(8,128)(2,1)} %all-gather.6.cloned.1.call-done) | data formatting | bytes 36700160
  462.1 15.7 %fusion.49 = (f32[1280]{0:T(1024)S(1)}, f32[1280,512]{1,0:T(8,128)S(1)}) fusion(bf16[1280,7168]{1,0:T(8,128)(2,1)} %reshape.70, bf16[512,7168]{1,0:T(8,128)(2,1)} %param.20), kind=kOutput, calls=%fused_computation.71 | convolution fusion | flops 9395895296 | bytes 28316672 | tf_op jit(solution)/shard_map/dot_general | solution.py:78
  477.8 0.2 reduce_max.26
  478.0 66.2 %all-reduce.3 = (f32[256,5]{1,0:T(8,128)S(1)}, f32[256,4]{1,0:T(8,128)S(1)}) all-reduce(f32[256,5]{1,0:T(8,128)S(1)} %reduce_max.26, bf16[256,4]{1,0:T(8,128)(2,1)S(1)} %reduce_max.27), channel_id=1, replica_groups=mesh['row'=4,'vocab'=32] {'row','vocab'}, use_global_device_ids=true, to_apply=%region_7.8 | all-reduce | flops 2304 | bytes 16384 | tf_op jit(solution)/shard_map/pmax | solution.py:95
  544.2 0.2 sub.62
  544.4 2.1 reshape.68
  546.6 0.9 exponential_reduce_fusion
  547.4 0.0 copy-start.4
  547.5 0.2 reduce_sum.96
  547.7 2.4 fusion.8
  550.0 65.6 %all-reduce.2 = (f32[256,5]{1,0:T(8,128)S(1)}, f32[256,4]{1,0:T(8,128)S(1)}) all-reduce(f32[256,5]{1,0:T(8,128)S(1)} %reduce_sum.96, f32[256,4]{1,0:T(8,128)S(1)} %fusion.8), channel_id=1, replica_groups=mesh['row'=4,'vocab'=32] {'row','vocab'}, use_global_device_ids=true, to_apply=%region_9.10 | all-reduce | flops 2304 | bytes 18432 | tf_op jit(solution)/shard_map/psum | solution.py:98
  615.7 3.8 multiply_reduce_fusion
  619.5 0.0 copy-start.1
  619.6 5.6 fusion.10
  625.2 0.1 fusion.28
  625.3 64.1 %all-reduce.1 = (f32[256]{0:T(256)S(1)}, f32[256,4]{1,0:T(8,128)S(1)}, f32[256,4]{1,0:T(8,128)S(1)}) all-reduce(f32[256]{0:T(256)S(1)} %fusion.28, f32[256,4]{1,0:T(8,128)} %get-tuple-element.12, f32[256,4]{1,0:T(8,128)S(1)} %get-tuple-element.10), channel_id=1, replica_groups=mesh['row'=4,'vocab'=32] {'row','vocab'}, use_global_device_ids=true, to_apply=%region_17.18 | all-reduce | flops 2304 | bytes 18432 | tf_op jit(solution)/shard_map/psum | solution.py:112
  689.4 0.1 fusion.32
  689.5 0.7 copy.44
  690.2 1.0 divide_sqrt_fusion
  (20 shorter events, 0.1 us)
Async XLA Ops:
  7.2 301.1 %copy-start = (bf16[7168,32]{0,1:T(8,128)(2,1)S(1)}, bf16[7168,32]{0,1:T(8,128)(2,1)}, u32[]{:S(2)}) copy-start(bf16[7168,32]{0,1:T(8,128)(2,1)} %param.14) | copy-start | bytes 1376260
  7.2 97.4 %all-gather.4.cloned.1.call-start = ((), (), s32[]{:S(2)}) async-start(), calls=%async_computation.2 | async-start | bytes 6881280 | tf_op jit(solution)/shard_map/all_gather | solution.py:54
  47.5 249.6 %all-reduce.6.cloned.1.call-start = ((), (), s32[]{:S(2)}) async-start(), calls=%async_computation.4 | async-start | bytes 14680064
  127.8 5.4 copy-start.5
  127.8 6.3 copy-start.12
  134.2 2.0 copy-start.6
  152.5 0.7 copy-start.13
  154.4 153.8 %copy-start.8 = (f32[7168]{0:T(1024)S(1)}, f32[7168]{0:T(1024)}, u32[]{:S(2)}) copy-start(f32[7168]{0:T(1024)} %param.13) | copy-start | bytes 86020
  300.6 36.7 %copy-start.9 = (f32[7168]{0:T(1024)S(1)}, f32[7168]{0:T(1024)}, u32[]{:S(2)}) copy-start(f32[7168]{0:T(1024)} %param.19) | copy-start | bytes 86020
  300.6 37.6 %copy-start.10 = (s32[256,4]{0,1:T(4,128)S(1)}, s32[256,4]{0,1:T(4,128)}, u32[]{:S(2)}) copy-start(s32[256,4]{0,1:T(4,128)} %param.22) | copy-start | bytes 12292
  300.6 38.4 %copy-start.3 = (bf16[256,4,512]{2,1,0:T(4,128)(2,1)S(1)}, bf16[256,4,512]{2,1,0:T(4,128)(2,1)}, u32[]{:S(2)}) copy-start(bf16[256,4,512]{2,1,0:T(4,128)(2,1)} %param.21) | copy-start | bytes 3145732
  300.6 38.9 %copy-start.11 = (s32[256]{0:T(256)S(1)}, s32[256]{0:T(256)}, u32[]{:S(2)}) copy-start(s32[256]{0:T(256)} %param.23) | copy-start | bytes 3076
  300.6 34.4 %all-to-all-start.1 = ((bf16[32,3,7168]{2,1,0:T(4,128)(2,1)}), bf16[32,3,7168]{2,1,0:T(4,128)(2,1)S(1)}, u32[]{:S(2)}, u32[]{:S(2)}) async-start(bf16[32,3,7168]{2,1,0:T(4,128)(2,1)} %constant_dynamic-slice_fusion), calls=%async_computation.1 | async-start | bytes 3670016 | tf_op jit(solution)/shard_map/all_to_all | solution.py:70
  308.0 125.9 %all-gather.6.cloned.1.call-start = ((), (), s32[]{:S(2)}) async-start(), calls=%async_computation.3 | async-start | bytes 29589504 | tf_op jit(solution)/shard_map/all_gather | solution.py:79
  547.4 72.1 %copy-start.4 = (bf16[256,4,512]{2,1,0:T(4,128)(2,1)S(1)}, bf16[256,4,512]{2,1,0:T(4,128)(2,1)}, u32[]{:S(2)}) copy-start(bf16[256,4,512]{2,1,0:T(4,128)(2,1)} %param.21) | copy-start | bytes 3145732
  547.4 72.1 %copy-start.7 = (s32[256,4]{1,0:T(8,128)S(1)}, s32[256,4]{1,0:T(8,128)}, u32[]{:S(2)}) copy-start(s32[256,4]{1,0:T(8,128)} %copy.43) | copy-start | bytes 12292
  615.7 3.9 copy-start.2
  619.5 71.7 %copy-start.1 = (bf16[7168,32]{0,1:T(8,128)(2,1)S(1)}, bf16[7168,32]{0,1:T(8,128)(2,1)}, u32[]{:S(2)}) copy-start(bf16[7168,32]{0,1:T(8,128)(2,1)} %param.14) | copy-start | bytes 1376260
Sparse Core Ops, SparseCore 0:
  47.6 56.8 all-gather.3
  152.7 144.4 all-reduce.5
  338.3 95.5 all-gather.5
where the time goes:
time: 700 us; the launch traced here: 698 us
  waiting for transfers between devices  319 us (46%)
  blocking collectives  230 us (33%)
  local copies, waits for them, and re-layouts  77.8 us (11%)
  matrix products  31.9 us (5%)
  other arithmetic  16.7 us (2%)
  between operations  14.7 us (2%)
  starting transfers between devices  7.89 us (1%)
    unnamed x4, waiting for transfers between devices  143 us
    all_gather x1, waiting for transfers between devices, body(): lax.all_gather(final_normed, ('row', 'vocab'), axis=0, tiled=True)  94.2 us
    pmax x1, blocking collectives, body(): lax.pmax((local_top_target, local_top_draft), ('row', 'vocab'))  66.2 us
    psum x1, blocking collectives, body(): lax.psum((local_sum_target, local_sum_draft, pick_target, pick_draft), ('...  65.6 us
    psum x1, blocking collectives, body(): gap_total = lax.psum(jnp.sum(gap_rows, axis=-1), ('row', 'vocab'))  64.1 us
    all_gather x1, waiting for transfers between devices, body(): shard_piece = lax.all_gather(received, 'row', axis=0, tiled=True)  56.8 us
    unnamed x33, local copies, waits for them, and re-layouts  35.8 us
    all_to_all x1, blocking collectives, body(): lax.all_to_all(send_buffer, 'vocab', split_axis=0, concat_axis=0, tiled=T...  33.8 us
  transfers between devices with their start and end apart: 4, of which 4 were waited for; matrix products, arithmetic and copies ran while one was open for 0% of the time, Pallas kernels for 0%

commit v1 on v0

v1 whole, which is shorter than its diff:
```python
import jax
import jax.numpy as jnp
import numpy as np
from jax import lax
from jax.sharding import Mesh
from jax.sharding import PartitionSpec as P

V = 65536
DRAFTS = 4

VOCAB_AXES = ("vz", "vx", "core")
ALL_AXES = ("row",) + VOCAB_AXES
RING_ORDER = ("core", "vx", "vz", "row")


def rms_norm(values, gain):
    return values * lax.rsqrt(jnp.mean(values * values, axis=-1, keepdims=True) + 1e-06) * gain


def tree_psum(values):
    for axis in RING_ORDER:
        values = lax.psum(values, axis)
    return values


def tree_pmax(values):
    for axis in RING_ORDER:
        values = lax.pmax(values, axis)
    return values


def body(
    tokens,
    norm_gain,
    router,
    routes,
    w_gate,
    w_up,
    w_down,
    head_gain,
    head,
    draft_logits,
    draft_tokens,
    reject_pos,
):
    vocab_count = 1
    for axis in VOCAB_AXES:
        vocab_count *= lax.axis_size(axis)
    row_count = lax.axis_size("row")
    rows_dev = tokens.shape[0]
    model_width = tokens.shape[1]
    top_k = routes.shape[1]
    experts = w_gate.shape[0] * vocab_count
    capacity = min(rows_dev, (rows_dev * top_k + experts - 1) // experts)
    local_vocab = head.shape[0]
    requests = draft_tokens.shape[0]
    slot_total = DRAFTS + 1
    offset = lax.axis_index(ALL_AXES) * local_vocab
    local_ids = draft_tokens - offset
    id_match = jnp.arange(local_vocab, dtype=jnp.int32)[None, None, :] == local_ids[:, :, None]

    draft_vals = draft_logits.astype(jnp.float32)
    top_draft = tree_pmax(jnp.max(draft_vals, axis=-1))
    draft_exp = jnp.exp(draft_vals - top_draft[:, :, None])
    sum_draft, pick_d = tree_psum(
        (jnp.sum(draft_exp, axis=-1), jnp.sum(jnp.where(id_match, draft_vals, 0.0), axis=-1))
    )

    resid_in = tokens.astype(jnp.float32)
    normed = rms_norm(resid_in, norm_gain).astype(jnp.bfloat16)
    scores = jax.nn.sigmoid(jnp.dot(normed, router, preferred_element_type=jnp.float32))
    member = routes[:, :, None] == jnp.arange(experts, dtype=jnp.int32)[None, None, :]
    chosen = jnp.any(member, axis=1)
    chosen_int = chosen.astype(jnp.int32)
    picked = chosen.astype(jnp.float32) * scores
    weights = 2.5 * picked / jnp.sum(picked, axis=1, keepdims=True)
    earlier = jnp.cumsum(chosen_int, axis=0) - chosen_int
    slot_ids = jnp.arange(capacity, dtype=jnp.int32)[None, :, None]
    selector = ((earlier.T[:, None, :] == slot_ids) & chosen.T[:, None, :]).astype(jnp.float32)
    send_buffer = jnp.einsum(
        "esr,rd->sed", selector.astype(jnp.bfloat16), normed, preferred_element_type=jnp.float32
    ).astype(jnp.bfloat16)
    gate_w = w_gate[0]
    up_w = w_up[0]
    down_w = w_down[0]
    received = lax.all_to_all(send_buffer, VOCAB_AXES, split_axis=1, concat_axis=1, tiled=True)
    shard_piece = lax.all_gather(received, "row", axis=1, tiled=True)
    flat_rows = shard_piece.reshape(-1, model_width)
    gate_out = jnp.dot(flat_rows, gate_w, preferred_element_type=jnp.float32)
    up_out = jnp.dot(flat_rows, up_w, preferred_element_type=jnp.float32)
    hidden = (jax.nn.silu(gate_out) * up_out).astype(jnp.bfloat16)
    down_out = jnp.dot(hidden, down_w, preferred_element_type=jnp.float32).astype(jnp.bfloat16)
    summed = lax.psum_scatter(
        down_out.reshape(shard_piece.shape),
        "row",
        scatter_dimension=1,
        tiled=True,
    )
    returned = lax.all_to_all(summed, VOCAB_AXES, split_axis=1, concat_axis=1, tiled=True)
    combine = selector * weights.T[:, None, :]
    moe_sum = jnp.einsum(
        "esr,sed->rd", combine, returned.astype(jnp.float32), precision=lax.Precision.HIGHEST
    )
    mixed_rows = resid_in + moe_sum
    final_normed = rms_norm(mixed_rows, head_gain).astype(jnp.bfloat16)
    gathered = lax.all_gather(final_normed, ALL_AXES, axis=0, tiled=False)
    logits = jnp.einsum("gtd,wd->gtw", gathered, head, preferred_element_type=jnp.float32)
    target_logits = logits.reshape(requests, slot_total, local_vocab)
    pick_target = jnp.sum(jnp.where(id_match, target_logits[:, :DRAFTS], 0.0), axis=-1)
    top_target = tree_pmax(jnp.max(target_logits, axis=-1))
    target_exp = jnp.exp(target_logits - top_target[:, :, None])
    sum_target, pick_t = tree_psum((jnp.sum(target_exp, axis=-1), pick_target))
    target = target_exp / sum_target[:, :, None]
    draft_prob = draft_exp / sum_draft[:, :, None]
    log_target = pick_t - top_target[:, :DRAFTS] - jnp.log(sum_target[:, :DRAFTS])
    log_draft = pick_d - top_draft - jnp.log(sum_draft)
    accept = jnp.exp(jnp.minimum(log_target - log_draft, 0.0))
    position = (jnp.arange(slot_total, dtype=jnp.int32)[None, :] == reject_pos[:, None]).astype(
        jnp.float32
    )
    target_at = jnp.sum(position[:, :, None] * target, axis=1)
    draft_at = jnp.sum(position[:, :DRAFTS, None] * draft_prob, axis=1)
    gap_rows = jnp.maximum(target_at - draft_at, 0.0)
    gap_total = tree_psum(jnp.sum(gap_rows, axis=-1))
    residual = jnp.sqrt(V * gap_rows / gap_total[:, None])
    return (residual, accept)


def solution(mesh):
    row_size, vocab_size = mesh.devices.shape
    split = (row_size, 4, vocab_size // 8, 2)
    fine = Mesh(np.asarray(mesh.devices).reshape(split), ALL_AXES)
    spread = ALL_AXES
    placed = (
        P(spread, None),
        P(),
        P(),
        P(spread, None),
        P(VOCAB_AXES, None, "row"),
        P(VOCAB_AXES, None, "row"),
        P(VOCAB_AXES, "row", None),
        P(),
        P(spread, None),
        P(None, None, spread),
        P(),
        P(),
    )
    return jax.shard_map(
        body,
        mesh=fine,
        in_specs=placed,
        out_specs=(P(None, spread), P()),
        check_vma=False,
    )
```

time: 700 us -> 655 us (0.936)
  local copies, waits for them, and re-layouts: 77.8 us -> 30.4 us
  matrix products: 31.9 us -> 48.6 us
  blocking collectives: 230 us -> 214 us
    unnamed x33 -> x32, local copies, waits for them, and re-layouts: 35.8 us -> 7.58 us
    dot_general x4, matrix products: 23.5 us -> 40.2 us  [the longest x1 32.4 us: body(): jnp.einsum('gtd,wd->gtw', gathered, head, preferred_element_type=jnp.floa...]
    convert_element_type x2 -> x1, local copies, waits for them, and re-layouts: 13.5 us -> 1.18 us  [body(): send_buffer = jnp.einsum('esr,rd->sed', selector.astype(jnp.bfloat16), no...]
    psum x2 -> x8, blocking collectives: 130 us -> 118 us  [tree_psum(): values = lax.psum(values, axis)]
    all_gather x1 -> x0, local copies, waits for them, and re-layouts: 10.2 us -> none  [body(): shard_piece = lax.all_gather(received, 'row', axis=0, tiled=True)]
    pmax x1 -> x4, blocking collectives: 66.2 us -> 62 us  [tree_pmax(): values = lax.pmax(values, axis)]
  transfers between devices with their start and end apart: 4 -> 4, of which waited for: 4 -> 4; matrix products, arithmetic and copies ran while one was open for 0% -> 1% of each run, Pallas kernels for 0% -> 0%
where the time goes in v1:
time: 655 us; the launch traced here: 651 us
  waiting for transfers between devices  319 us (49%)
  blocking collectives  214 us (33%)
  matrix products  48.6 us (7%)
  local copies, waits for them, and re-layouts  30.4 us (5%)
  other arithmetic  16.4 us (3%)
  between operations  14.9 us (2%)
  starting transfers between devices  7.67 us (1%)
    unnamed x4, waiting for transfers between devices  143 us
    psum x8, blocking collectives, tree_psum(): values = lax.psum(values, axis)  118 us
    all_gather x1, waiting for transfers between devices, body(): gathered = lax.all_gather(final_normed, ALL_AXES, axis=0, tiled=False)  94.2 us
    pmax x4, blocking collectives, tree_pmax(): values = lax.pmax(values, axis)  62 us
    all_gather x1, waiting for transfers between devices, body(): shard_piece = lax.all_gather(received, 'row', axis=1, tiled=True)  56.8 us
    all_to_all x1, blocking collectives, body(): lax.all_to_all(send_buffer, VOCAB_AXES, split_axis=1, concat_axis=1, tile...  33.8 us
    dot_general x1, matrix products, body(): jnp.einsum('gtd,wd->gtw', gathered, head, preferred_element_type=jnp.floa...  32.4 us
    all_to_all x1, waiting for transfers between devices, body(): lax.all_to_all(summed, VOCAB_AXES, split_axis=1, concat_axis=1, tiled=True)  25.5 us
  transfers between devices with their start and end apart: 4, of which 4 were waited for; matrix products, arithmetic and copies ran while one was open for 1% of the time, Pallas kernels for 0%

profile of v1, /device:TPU:0, one launch (start us, length us, event | category | flops | bytes accessed | tf_op | source)
XLA Modules:
  0.0 651.2 jit_solution(5099887849405684737)
XLA Ops:
  7.2 0.0 copy-start
  7.2 0.0 all-gather.5.cloned.1.call-start
  7.2 0.8 copy.62
  8.0 0.1 fusion.40
  8.2 1.1 fusion.27
  9.3 1.5 fusion.2
  10.8 1.2 copy.63
  12.0 33.8 %all_to_all.10 = bf16[3,32,7168]{2,0,1:T(4,128)(2,1)S(1)} all-to-all(bf16[3,32,7168]{2,0,1:T(4,128)(2,1)S(1)} %copy.63), channel_id=1, replica_groups=mesh['row'=4,'vz'=4,'vx'=4,'core'=2] {'vz','vx','core'}, dimensions={1} | all-to-all | bytes 2752512 | tf_op jit(solution)/shard_map/all_to_all | solution.py:86
  45.8 1.7 copy.64
  47.5 0.0 all-gather.5.cloned.1.call-update
  47.5 0.2 all-reduce.15.cloned.1.call-start
  47.8 56.8 %all-gather.5.cloned.1.call-done = bf16[3,128,7168]{2,1,0:T(8,128)(2,1)} async-done(((bf16[3,32,7168]{2,1,0:T(8,128)(2,1)}), bf16[3,128,7168]{2,1,0:T(8,128)(2,1)}) %all-gather.5.cloned.1.call-update) | async-done | bytes 5505040 | tf_op jit(solution)/shard_map/all_gather | solution.py:87
  104.6 5.4 fusion.8
  110.0 0.9 copy-done.12
  110.9 1.6 fusion.21
  112.5 0.4 copy-done.5
  113.0 4.0 convolution_convert_fusion
  117.0 10.3 %copy.65 = bf16[3,128,7168]{2,0,1:T(4,128)(2,1)} copy(bf16[3,128,7168]{2,1,0:T(8,128)(2,1)} %bitcast.48) | data formatting | bytes 11010048 | tf_op jit(solution)/shard_map/reshape | solution.py:94
  127.3 0.0 all-reduce.15.cloned.1.call-update
  127.3 0.6 copy-done.13
  127.9 0.6 dynamic-slice
  129.2 142.7 %all-reduce.15.cloned.1.call-done = bf16[3,128,7168]{2,0,1:T(4,128)(2,1)} async-done(((bf16[3,128,7168]{2,0,1:T(4,128)(2,1)}), bf16[3,128,7168]{2,0,1:T(4,128)(2,1)}) %all-reduce.15.cloned.1.call-update) | async-done | bytes 5505040
  271.9 3.5 constant_dynamic-slice_fusion
  275.3 7.4 %all-to-all-start.1 = ((bf16[3,32,7168]{2,0,1:T(4,128)(2,1)}), bf16[3,32,7168]{2,0,1:T(4,128)(2,1)S(1)}, u32[]{:S(2)}, u32[]{:S(2)}) async-start(bf16[3,32,7168]{2,0,1:T(4,128)(2,1)} %constant_dynamic-slice_fusion), calls=%async_computation.1 | async-start | bytes 3670016 | tf_op jit(solution)/shard_map/all_to_all | solution.py:99
  282.7 0.0 all-gather.7.cloned.1.call-start
  282.8 1.4 select_reduce_fusion
  284.2 0.1 fusion.51
  284.2 25.5 %all-to-all-done.1 = bf16[3,32,7168]{2,0,1:T(4,128)(2,1)S(1)} async-done(((bf16[3,32,7168]{2,0,1:T(4,128)(2,1)}), bf16[3,32,7168]{2,0,1:T(4,128)(2,1)S(1)}, u32[]{:S(2)}, u32[]{:S(2)}) %all-to-all-start.1) | async-done | bytes 1376288 | tf_op jit(solution)/shard_map/all_to_all | solution.py:99
  309.7 2.3 multiply_reduce_fusion.1
  312.1 0.8 fusion.30
  312.9 0.0 all-gather.7.cloned.1.call-update
  312.9 0.8 copy.72
  313.7 0.5 reduce_max.27
  314.2 0.1 fusion.37
  314.4 94.2 %all-gather.7.cloned.1.call-done = bf16[128,10,7168]{2,1,0:T(8,128)(2,1)} async-done(((bf16[1,10,7168]{2,1,0:T(8,128)(2,1)}), bf16[128,10,7168]{2,1,0:T(8,128)(2,1)}) %all-gather.7.cloned.1.call-update) | async-done | bytes 18350096 | tf_op jit(solution)/shard_map/all_gather | solution.py:106
  408.6 32.4 %fusion.53 = (f32[128,10]{0,1:T(8,128)S(1)}, f32[128,10,512]{2,0,1:T(8,128)S(1)}) fusion(bf16[512,7168]{1,0:T(8,128)(2,1)} %param.20, bf16[128,10,7168]{2,1,0:T(8,128)(2,1)} %all-gather.7.cloned.1.call-done), kind=kOutput, calls=%fused_computation.75 | convolution fusion | flops 9395895296 | bytes 28316672 | tf_op jit(solution)/shard_map/gtd,wd->gtw/dot_general | solution.py:107
  441.0 0.1 copy.69
  441.1 0.1 reduce_max.26
  441.2 4.2 all-reduce.12
  445.4 20.1 %all-reduce.7 = (f32[256,5]{1,0:T(8,128)S(1)}, f32[256,4]{1,0:T(8,128)S(1)}) all-reduce(f32[256,5]{1,0:T(8,128)S(1)} %get-tuple-element.41, f32[256,4]{1,0:T(8,128)S(1)} %get-tuple-element.42), channel_id=1, replica_groups=mesh['row'=4,'vz'=4,'vx'=4,'core'=2] {'vx'}, use_global_device_ids=true, to_apply=%region_8.9 | all-reduce | flops 2304 | bytes 18432 | tf_op jit(solution)/shard_map/pmax | solution.py:28
  465.6 18.6 %all-reduce.8 = (f32[256,5]{1,0:T(8,128)S(1)}, f32[256,4]{1,0:T(8,128)S(1)}) all-reduce(f32[256,5]{1,0:T(8,128)S(1)} %get-tuple-element.30, f32[256,4]{1,0:T(8,128)S(1)} %get-tuple-element.31), channel_id=1, replica_groups=mesh['row'=4,'vz'=4,'vx'=4,'core'=2] {'vz'}, use_global_device_ids=true, to_apply=%region_9.10 | all-reduce | flops 2304 | bytes 18432 | tf_op jit(solution)/shard_map/pmax | solution.py:28
  484.2 19.0 %all-reduce.9 = (f32[256,5]{1,0:T(8,128)S(1)}, f32[256,4]{1,0:T(8,128)S(1)}) all-reduce(f32[256,5]{1,0:T(8,128)S(1)} %get-tuple-element.32, f32[256,4]{1,0:T(8,128)S(1)} %get-tuple-element.33), channel_id=1, replica_groups=mesh['row'=4,'vz'=4,'vx'=4,'core'=2] {'row'}, use_global_device_ids=true, to_apply=%region_10.11 | all-reduce | flops 2304 | bytes 18432 | tf_op jit(solution)/shard_map/pmax | solution.py:28
  503.3 0.1 sub.54
  503.3 0.1 copy.70
  503.4 3.6 copy.68
  507.0 0.7 exponential_reduce_fusion
  507.7 0.1 copy.71
  507.8 0.1 reduce_sum.96
  507.9 2.3 fusion.12
  510.2 4.8 reshape.70
  514.9 4.1 all-reduce.11
  519.1 18.1 %all-reduce.2 = (f32[256,5]{1,0:T(8,128)S(1)}, f32[256,4]{1,0:T(8,128)S(1)}) all-reduce(f32[256,5]{1,0:T(8,128)S(1)} %get-tuple-element.39, f32[256,4]{1,0:T(8,128)S(1)} %get-tuple-element.40), channel_id=1, replica_groups=mesh['row'=4,'vz'=4,'vx'=4,'core'=2] {'vx'}, use_global_device_ids=true, to_apply=%region_13.14 | all-reduce | flops 2304 | bytes 18432 | tf_op jit(solution)/shard_map/psum | solution.py:22
  537.2 17.8 %all-reduce.4 = (f32[256,5]{1,0:T(8,128)S(1)}, f32[256,4]{1,0:T(8,128)S(1)}) all-reduce(f32[256,5]{1,0:T(8,128)S(1)} %get-tuple-element.18, f32[256,4]{1,0:T(8,128)S(1)} %get-tuple-element.19), channel_id=1, replica_groups=mesh['row'=4,'vz'=4,'vx'=4,'core'=2] {'vz'}, use_global_device_ids=true, to_apply=%region_14.15 | all-reduce | flops 2304 | bytes 18432 | tf_op jit(solution)/shard_map/psum | solution.py:22
  555.0 17.0 %all-reduce.6 = (f32[256,5]{1,0:T(8,128)S(1)}, f32[256,4]{1,0:T(8,128)S(1)}) all-reduce(f32[256,5]{1,0:T(8,128)S(1)} %get-tuple-element.23, f32[256,4]{1,0:T(8,128)S(1)} %get-tuple-element.24), channel_id=1, replica_groups=mesh['row'=4,'vz'=4,'vx'=4,'core'=2] {'row'}, use_global_device_ids=true, to_apply=%region_15.16 | all-reduce | flops 2304 | bytes 18432 | tf_op jit(solution)/shard_map/psum | solution.py:22
  572.0 3.8 multiply_reduce_fusion
  575.9 5.6 fusion.14
  581.6 0.1 fusion.32
  581.7 4.7 all-reduce.10
  586.4 20.3 %all-reduce.1 = (f32[256]{0:T(256)S(1)}, f32[256,4]{1,0:T(8,128)S(1)}, f32[256,4]{1,0:T(8,128)S(1)}) all-reduce(f32[256]{0:T(256)S(1)} %get-tuple-element.36, f32[256,4]{1,0:T(8,128)S(1)} %get-tuple-element.37, f32[256,4]{1,0:T(8,128)S(1)} %get-tuple-element.38), channel_id=1, replica_groups=mesh['row'=4,'vz'=4,'vx'=4,'core'=2] {'vx'}, use_global_device_ids=true, to_apply=%region_30.31 | all-reduce | flops 2304 | bytes 18432 | tf_op jit(solution)/shard_map/psum | solution.py:22
  606.7 17.1 %all-reduce.3 = (f32[256]{0:T(256)S(1)}, f32[256,4]{1,0:T(8,128)S(1)}, f32[256,4]{1,0:T(8,128)S(1)}) all-reduce(f32[256]{0:T(256)S(1)} %get-tuple-element.15, f32[256,4]{1,0:T(8,128)S(1)} %get-tuple-element.16, f32[256,4]{1,0:T(8,128)S(1)} %get-tuple-element.17), channel_id=1, replica_groups=mesh['row'=4,'vz'=4,'vx'=4,'core'=2] {'vz'}, use_global_device_ids=true, to_apply=%region_31.32 | all-reduce | flops 2304 | bytes 18432 | tf_op jit(solution)/shard_map/psum | solution.py:22
  623.8 18.9 %all-reduce.5 = (f32[256]{0:T(256)S(1)}, f32[256,4]{1,0:T(8,128)S(1)}, f32[256,4]{1,0:T(8,128)S(1)}) all-reduce(f32[256]{0:T(256)S(1)} %get-tuple-element.20, f32[256,4]{1,0:T(8,128)S(1)} %get-tuple-element.21, f32[256,4]{1,0:T(8,128)S(1)} %get-tuple-element.22), channel_id=1, replica_groups=mesh['row'=4,'vz'=4,'vx'=4,'core'=2] {'row'}, use_global_device_ids=true, to_apply=%region_32.33 | all-reduce | flops 2304 | bytes 18432 | tf_op jit(solution)/shard_map/psum | solution.py:22
  642.7 0.1 fusion.36
  642.8 0.7 copy.73
  643.5 1.0 divide_sqrt_fusion
  (30 shorter events, 0.1 us)
Async XLA Ops:
  7.2 275.6 %copy-start = (bf16[7168,32]{0,1:T(8,128)(2,1)S(1)}, bf16[7168,32]{0,1:T(8,128)(2,1)}, u32[]{:S(2)}) copy-start(bf16[7168,32]{0,1:T(8,128)(2,1)} %param.14) | copy-start | bytes 1376260
  7.2 97.4 %all-gather.5.cloned.1.call-start = ((), (), s32[]{:S(2)}) async-start(), calls=%async_computation.2 | async-start | bytes 6881280 | tf_op jit(solution)/shard_map/all_gather | solution.py:87
  47.5 224.3 %all-reduce.15.cloned.1.call-start = ((), (), s32[]{:S(2)}) async-start(), calls=%async_computation.4 | async-start | bytes 14680064
  104.6 5.4 copy-start.11
  104.6 6.3 copy-start.12
  110.9 2.0 copy-start.5
  127.3 0.7 copy-start.13
  129.2 153.6 %copy-start.7 = (f32[7168]{0:T(1024)S(1)}, f32[7168]{0:T(1024)}, u32[]{:S(2)}) copy-start(f32[7168]{0:T(1024)} %param.13) | copy-start | bytes 86020
  275.3 36.7 %copy-start.8 = (f32[7168]{0:T(1024)S(1)}, f32[7168]{0:T(1024)}, u32[]{:S(2)}) copy-start(f32[7168]{0:T(1024)} %param.19) | copy-start | bytes 86020
  275.3 37.6 %copy-start.9 = (s32[256,4]{0,1:T(4,128)S(1)}, s32[256,4]{0,1:T(4,128)}, u32[]{:S(2)}) copy-start(s32[256,4]{0,1:T(4,128)} %param.22) | copy-start | bytes 12292
  275.3 38.4 %copy-start.3 = (bf16[256,4,512]{2,1,0:T(4,128)(2,1)S(1)}, bf16[256,4,512]{2,1,0:T(4,128)(2,1)}, u32[]{:S(2)}) copy-start(bf16[256,4,512]{2,1,0:T(4,128)(2,1)} %param.21) | copy-start | bytes 3145732
  275.3 38.9 %copy-start.10 = (s32[256]{0:T(256)S(1)}, s32[256]{0:T(256)}, u32[]{:S(2)}) copy-start(s32[256]{0:T(256)} %param.23) | copy-start | bytes 3076
  275.3 34.4 %all-to-all-start.1 = ((bf16[3,32,7168]{2,0,1:T(4,128)(2,1)}), bf16[3,32,7168]{2,0,1:T(4,128)(2,1)S(1)}, u32[]{:S(2)}, u32[]{:S(2)}) async-start(bf16[3,32,7168]{2,0,1:T(4,128)(2,1)} %constant_dynamic-slice_fusion), calls=%async_computation.1 | async-start | bytes 3670016 | tf_op jit(solution)/shard_map/all_to_all | solution.py:99
  282.7 125.9 %all-gather.7.cloned.1.call-start = ((), (), s32[]{:S(2)}) async-start(), calls=%async_computation.3 | async-start | bytes 29589504 | tf_op jit(solution)/shard_map/all_gather | solution.py:106
  514.9 61.0 %copy-start.4 = (bf16[256,4,512]{2,1,0:T(4,128)(2,1)S(1)}, bf16[256,4,512]{2,1,0:T(4,128)(2,1)}, u32[]{:S(2)}) copy-start(bf16[256,4,512]{2,1,0:T(4,128)(2,1)} %param.21) | copy-start | bytes 3145732
  514.9 61.0 %copy-start.6 = (s32[256,4]{1,0:T(8,128)S(1)}, s32[256,4]{1,0:T(8,128)}, u32[]{:S(2)}) copy-start(s32[256,4]{1,0:T(8,128)} %copy.72) | copy-start | bytes 12292
  572.0 3.9 copy-start.2
  575.9 68.6 %copy-start.1 = (bf16[7168,32]{0,1:T(8,128)(2,1)S(1)}, bf16[7168,32]{0,1:T(8,128)(2,1)}, u32[]{:S(2)}) copy-start(bf16[7168,32]{0,1:T(8,128)(2,1)} %param.14) | copy-start | bytes 1376260
Sparse Core Ops, SparseCore 0:
  47.7 56.8 all-gather.4
  127.4 144.4 all-reduce.14
  313.0 95.5 all-gather.6
